TPU v7x, 128 devices: a whole 4x4x4 slice. The times are simulated.
128 devices in a mesh: ang: 64 (over x, y_lo, z, core), pix: 2 (over y_hi).
Axes of the slice: x: 4, y: 4 (y_hi: 2, y_lo: 2; y = y_hi * 2 + y_lo), z: 4, core: 2. Of those that a mesh axis runs over, the one named last changes fastest.
Arguments:
- grads: bfloat16 [2, 4096, 128, 512], P(None, 'ang', 'pix')
- circle_pos: int32 [4096], replicated, may hold values from 0 to 4095, as said below
- harmonics: int32 [256], replicated, may hold values from 0 to 4095, as said below
- support: int32 [128, 512], replicated, may hold values 0 or 1
Outputs:
- update: bfloat16 [2, 4096, 128, 512], P(None, 'ang', 'pix')
- harmonic_rms: float32 [256], replicated
Inputs may be any that keep to these rules, and one draw needn't show every extreme that they name: `circle_pos`: the stored angles form 64 aligned blocks of 64 rows; block b holds the circle positions r_b + 64 * j for j = 0 to 63 in this order, and the 64 values r_b are distinct. `harmonics`: 256 distinct harmonic numbers, among them 0 and 4095.
All inputs are finite; a program needn't handle non-finite values.
Results may differ from a plain program's by a relative error of at most 0.015.
Values may be sent and summed in bfloat16 or wider, within the bound.
No kernel may reach another device: no remote copies, remote signals or barrier semaphores. Data moves between devices by JAX's collectives and lax.ppermute only.
A program may use at most 192 MiB of HBM per device.

v0:
```python
import math
import jax
import jax.numpy as jnp
from jax import lax
from jax.sharding import PartitionSpec as P


def phase_pair(product, modulus):
    radians = (product % modulus).astype(jnp.float32) * (2.0 * math.pi / modulus)
    return (jnp.cos(radians), jnp.sin(radians))


def split_parts(value):
    if value.dtype == jnp.bfloat16:
        return (value,)
    high = value.astype(jnp.bfloat16)
    low = (value - high.astype(jnp.float32)).astype(jnp.bfloat16)
    return (high, low)


def split_einsum(form, left, right):
    left_parts = split_parts(left)
    right_parts = split_parts(right)
    total = None
    for left_rank, left_piece in enumerate(left_parts):
        for right_rank, right_piece in enumerate(right_parts):
            if left_rank + right_rank <= 1:
                term = jnp.einsum(form, left_piece, right_piece, preferred_element_type=jnp.float32)
                total = term if total is None else total + term
    return total


def normalize(coef_re, coef_im, weight, cell_count):
    square_sums = jnp.sum(weight[None, :] * (coef_re * coef_re + coef_im * coef_im), axis=1)
    totals = lax.psum(square_sums, ("ang", "pix"))
    harmonic_rms = jnp.sqrt(totals / cell_count + 1e-06)
    factor = weight[None, :] / harmonic_rms[:, None]
    return (coef_re * factor, coef_im * factor, harmonic_rms)


def direct_path(grads, circle_pos, harmonics, weight, cell_count):
    angle_count = circle_pos.shape[0]
    kept_count = harmonics.shape[0]
    moved = lax.all_to_all(grads, "ang", split_axis=2, concat_axis=1, tiled=True)
    row_local = moved.shape[2]
    col_count = moved.shape[3]
    flat = moved.reshape(2, angle_count, row_local * col_count)
    pixel_count = flat.shape[2]
    phase_cos, phase_sin = phase_pair(harmonics[:, None] * circle_pos[None, :], angle_count)
    table = jnp.concatenate((phase_cos, phase_sin), 0)
    products = split_einsum("ka,ap->kp", table, jnp.concatenate((flat[0], flat[1]), 1))
    scale = 1.0 / math.sqrt(angle_count)
    coef_re = (products[:kept_count, :pixel_count] + products[kept_count:, pixel_count:]) * scale
    coef_im = (products[:kept_count, pixel_count:] - products[kept_count:, :pixel_count]) * scale
    step_re, step_im, harmonic_rms = normalize(coef_re, coef_im, weight, cell_count)
    right_side = jnp.concatenate(
        (jnp.concatenate((step_re, -step_im), 0), jnp.concatenate((step_im, step_re), 0)), 1
    )
    synthesis = split_einsum("ka,kp->ap", table, right_side)
    scale_back = 1.0 / math.sqrt(kept_count)
    update = jnp.stack((synthesis[:, :pixel_count], synthesis[:, pixel_count:])) * scale_back
    update = update.astype(jnp.bfloat16).reshape(2, angle_count, row_local, col_count)
    return (lax.all_to_all(update, "ang", split_axis=1, concat_axis=2, tiled=True), harmonic_rms)


def body(grads, circle_pos, harmonics, support):
    ang_count = lax.axis_size("ang")
    row_pix = grads.shape[2]
    row_local = row_pix // ang_count
    col_count = grads.shape[3]
    row_start = lax.axis_index("pix") * row_pix + lax.axis_index("ang") * row_local
    weight = (
        lax.dynamic_slice_in_dim(support, row_start, row_local, 0).astype(jnp.float32).reshape(-1)
    )
    cell_count = float(row_pix * lax.axis_size("pix") * col_count)
    update, harmonic_rms = direct_path(grads, circle_pos, harmonics, weight, cell_count)
    return (update, harmonic_rms)


def solution(mesh):
    placed = (P(None, "ang", "pix", None), P(), P(), P())
    return jax.shard_map(
        body,
        mesh=mesh,
        in_specs=placed,
        out_specs=(P(None, "ang", "pix", None), P()),
        check_vma=False,
    )
```

profile of v0, /device:TPU:1, one launch (start us, length us, event | category | flops | bytes accessed | tf_op | source)
XLA Modules:
  0.0 437.9 jit_solution(5942899219189294290)
XLA Ops:
  0.6 11.5 %copy.18 = bf16[2,64,64,512]{3,1,0,2:T(8,128)(2,1)} copy(bf16[2,64,64,512]{3,2,1,0:T(8,128)(2,1)} %param.4) | data formatting | bytes 16777216 | tf_op args[0]
  12.1 0.0 copy-start.6
  12.1 0.0 copy-start.8
  12.1 11.2 %all-to-all-start = ((bf16[2,64,64,512]{3,1,0,2:T(8,128)(2,1)}), bf16[2,64,64,512]{3,1,0,2:T(8,128)(2,1)}, u32[]{:S(2)}, u32[]{:S(2)}) async-start(bf16[2,64,64,512]{3,1,0,2:T(8,128)(2,1)} %copy.18), calls=%async_computation | async-start | bytes 16777216 | tf_op jit(solution)/shard_map/all_to_all | solution.py:44
  23.3 0.7 dynamic-slice_convert_fusion
  24.1 0.0 copy-done.6
  24.1 0.0 copy-done.8
  24.1 18.0 %fusion.8 = (f32[256,4096]{1,0:T(8,128)}, f32[256,4096]{1,0:T(8,128)}) fusion(s32[4096]{0:T(1024)S(1)} %copy-done.6, s32[256]{0:T(256)S(1)} %copy-done.8), kind=kLoop, calls=%fused_computation.23 | loop fusion | flops 14680064 | bytes 8406016 | tf_op jit(solution)/shard_map/cos | solution.py:10
  42.1 84.6 %all-to-all-done = bf16[2,64,64,512]{3,1,0,2:T(8,128)(2,1)} async-done(((bf16[2,64,64,512]{3,1,0,2:T(8,128)(2,1)}), bf16[2,64,64,512]{3,1,0,2:T(8,128)(2,1)}, u32[]{:S(2)}, u32[]{:S(2)}) %all-to-all-start) | async-done | bytes 8388640 | tf_op jit(solution)/shard_map/all_to_all | solution.py:44
  126.7 7.9 %copy.24 = bf16[2,64,64,512]{3,1,2,0:T(8,128)(2,1)} copy(bf16[2,64,64,512]{3,1,0,2:T(8,128)(2,1)} %all-to-all-done) | data formatting | bytes 16777216 | tf_op jit(solution)/shard_map/all_to_all | solution.py:44
  134.6 0.0 copy-start
  134.6 0.0 copy-start.2
  134.6 5.4 %fusion.27 = (bf16[1,64,64,1,512]{4,2,1,3,0:T(8,128)(2,1)S(1)}, bf16[1,64,64,1,512]{4,2,1,3,0:T(8,128)(2,1)}) fusion(bf16[2,64,64,1,512]{4,2,1,3,0:T(8,128)(2,1)} %bitcast.17), kind=kLoop, calls=%fused_computation.41 | loop fusion | bytes 16777216 | tf_op jit(solution)/shard_map/slice | solution.py:51
  140.0 0.0 copy-start.5
  140.0 2.1 copy-done.5
  142.1 0.0 copy-done
  142.1 1.5 copy-done.2
  143.6 8.0 %fusion.2 = f32[512,1024]{1,0:T(8,128)} fusion(bf16[4096,512]{1,0:T(8,128)(2,1)} %bitcast.21, bf16[4096,512]{1,0:T(8,128)(2,1)S(1)} %bitcast.19, f32[256,4096]{1,0:T(8,128)S(1)} %copy-done.2, f32[256,4096]{1,0:T(8,128)S(1)} %copy-done), kind=kOutput, calls=%fused_computation.15 | convolution fusion | flops 4322230272 | bytes 18874368 | tf_op jit(solution)/shard_map/ka,ap->kp/dot_general | solution.py:28
  151.6 8.5 %fusion.9 = f32[512,1024]{1,0:T(8,128)S(1)} fusion(f32[512,1024]{1,0:T(8,128)} %fusion.2, bf16[4096,512]{1,0:T(8,128)(2,1)} %bitcast.22, bf16[4096,512]{1,0:T(8,128)(2,1)} %bitcast.20, f32[256,4096]{1,0:T(8,128)S(1)} %copy-done.2, f32[256,4096]{1,0:T(8,128)S(1)} %copy-done), kind=kOutput, calls=%fused_computation.24 | convolution fusion | flops 4320657408 | bytes 20971520 | tf_op jit(solution)/shard_map/ka,ap->kp/dot_general | solution.py:28
  160.1 0.0 copy-start.4
  160.2 1.3 copy-done.4
  161.5 0.2 multiply_reduce_fusion
  161.7 70.5 %psum.7 = f32[256]{0:T(256)S(1)} all-reduce(f32[256]{0:T(256)S(1)} %multiply_reduce_fusion), channel_id=1, replica_groups=mesh['ang'=64,'pix'=2] {'ang','pix'}, use_global_device_ids=true, to_apply=%region_1.2 | all-reduce | flops 256 | bytes 2048 | tf_op jit(solution)/shard_map/psum | solution.py:35
  232.2 0.0 copy-start.7
  232.3 1.7 fusion.26
  234.0 0.0 copy-start.1
  234.0 0.0 copy-start.3
  234.0 12.7 %fusion.11 = f32[4096,1024]{1,0:T(8,128)} fusion(f32[256,512]{1,0:T(8,128)S(1)} %get-tuple-element.12, f32[256,512]{1,0:T(8,128)S(1)} %get-tuple-element.7, f32[256,512]{1,0:T(8,128)S(1)} %get-tuple-element.6, f32[256,4096]{1,0:T(8,128)} %get-tuple-element.14, f32[256,4096]{1,0:T(8,128)} %get-tuple-element.13), kind=kOutput, calls=%fused_computation.26 | convolution fusion | flops 4307025920 | bytes 26738688 | tf_op jit(solution)/shard_map/ka,kp->ap/dot_general | solution.py:28
  246.7 0.0 copy-done.7
  246.7 0.0 copy-done.1
  246.7 0.0 copy-done.3
  246.7 8.2 %fusion.19 = f32[4096,1024]{1,0:T(8,128)} fusion(f32[256,512]{1,0:T(8,128)S(1)} %get-tuple-element.12, f32[256,512]{1,0:T(8,128)S(1)} %get-tuple-element.7, f32[256,512]{1,0:T(8,128)S(1)} %get-tuple-element.6, f32[256,4096]{1,0:T(8,128)S(1)} %copy-done.3, f32[256,4096]{1,0:T(8,128)S(1)} %copy-done.1), kind=kOutput, calls=%fused_computation.39 | convolution fusion | flops 4307550208 | bytes 26738688 | tf_op jit(solution)/shard_map/ka,kp->ap/dot_general | solution.py:28
  254.9 19.3 %add_add_fusion = f32[4096,1024]{1,0:T(8,128)} fusion(f32[4096,1024]{1,0:T(8,128)} %fusion.19, f32[4096,1024]{1,0:T(8,128)} %fusion.11, f32[256,512]{1,0:T(8,128)S(1)} %get-tuple-element.12, f32[256,512]{1,0:T(8,128)S(1)} %get-tuple-element.7, f32[256,512]{1,0:T(8,128)S(1)} %get-tuple-element.6, f32[256,4096]{1,0:T(8,128)} %get-tuple-element.14, ...), kind=kOutput, calls=%fused_computation.2 | convolution fusion | flops 4318035968 | bytes 60293120 | tf_op jit(solution)/shard_map/ka,kp->ap/dot_general | solution.py:28
  274.1 6.9 %slice_bitcast_fusion.1 = (f32[1,4096,1,512]{3,1,2,0:T(8,128)S(1)}, f32[1,4096,1,512]{3,1,2,0:T(8,128)S(1)}) fusion(f32[4096,1024]{1,0:T(8,128)} %add_add_fusion), kind=kLoop, calls=%fused_computation.4 | loop fusion | bytes 33554432 | tf_op jit(solution)/shard_map/stack | solution.py:61
  281.0 2.5 fusion
  283.5 32.6 %copy.20 = bf16[2,4096,1,512]{3,0,2,1:T(2,128)(2,1)S(1)} copy(bf16[2,4096,1,512]{3,1,2,0:T(8,128)(2,1)S(1)} %fusion) | data formatting | bytes 16777216 | tf_op jit(solution)/shard_map/convert_element_type | solution.py:62
  316.2 102.3 %all_to_all.33 = bf16[2,4096,1,512]{3,0,2,1:T(2,128)(2,1)} all-to-all(bf16[2,4096,1,512]{3,0,2,1:T(2,128)(2,1)S(1)} %copy.20), channel_id=1, replica_groups=mesh['ang'=64,'pix'=2] {'ang'}, dimensions={1} | all-to-all | bytes 16777216 | tf_op jit(solution)/shard_map/all_to_all | solution.py:63
  418.4 8.0 %copy.21 = bf16[2,4096,1,512]{3,1,0,2:T(8,128)(2,1)} copy(bf16[2,4096,1,512]{3,0,2,1:T(2,128)(2,1)} %all_to_all.33) | data formatting | bytes 16777216 | tf_op jit(solution)/shard_map/all_to_all | solution.py:63
  426.4 11.5 %copy.22 = bf16[2,64,64,512]{3,2,1,0:T(8,128)(2,1)} copy(bf16[2,64,64,512]{3,1,2,0:T(8,128)(2,1)} %bitcast.18) | data formatting | bytes 16777216
  (1 shorter events, 0.0 us)
Async XLA Ops:
  12.1 11.9 %copy-start.6 = (s32[4096]{0:T(1024)S(1)}, s32[4096]{0:T(1024)}, u32[]{:S(2)}) copy-start(s32[4096]{0:T(1024)} %param.5) | copy-start | bytes 49156
  12.1 11.9 %copy-start.8 = (s32[256]{0:T(256)S(1)}, s32[256]{0:T(256)}, u32[]{:S(2)}) copy-start(s32[256]{0:T(256)} %param.6) | copy-start | bytes 3076
  12.1 114.6 %all-to-all-start = ((bf16[2,64,64,512]{3,1,0,2:T(8,128)(2,1)}), bf16[2,64,64,512]{3,1,0,2:T(8,128)(2,1)}, u32[]{:S(2)}, u32[]{:S(2)}) async-start(bf16[2,64,64,512]{3,1,0,2:T(8,128)(2,1)} %copy.18), calls=%async_computation | async-start | bytes 16777216 | tf_op jit(solution)/shard_map/all_to_all | solution.py:44
  134.6 7.5 %copy-start = (f32[256,4096]{1,0:T(8,128)S(1)}, f32[256,4096]{1,0:T(8,128)}, u32[]{:S(2)}) copy-start(f32[256,4096]{1,0:T(8,128)} %get-tuple-element.13) | copy-start | bytes 12582916
  134.6 9.0 %copy-start.2 = (f32[256,4096]{1,0:T(8,128)S(1)}, f32[256,4096]{1,0:T(8,128)}, u32[]{:S(2)}) copy-start(f32[256,4096]{1,0:T(8,128)} %get-tuple-element.14) | copy-start | bytes 12582916
  140.0 2.1 copy-start.5
  160.1 1.3 copy-start.4
  232.2 14.4 %copy-start.7 = (f32[256]{0:T(256)}, f32[256]{0:T(256)S(1)}, u32[]{:S(2)}) copy-start(f32[256]{0:T(256)S(1)} %add_sqrt_fusion) | copy-start | bytes 3076
  234.0 12.7 %copy-start.1 = (f32[256,4096]{1,0:T(8,128)S(1)}, f32[256,4096]{1,0:T(8,128)}, u32[]{:S(2)}) copy-start(f32[256,4096]{1,0:T(8,128)} %get-tuple-element.13) | copy-start | bytes 12582916
  234.0 12.7 %copy-start.3 = (f32[256,4096]{1,0:T(8,128)S(1)}, f32[256,4096]{1,0:T(8,128)}, u32[]{:S(2)}) copy-start(f32[256,4096]{1,0:T(8,128)} %get-tuple-element.14) | copy-start | bytes 12582916
where the time goes:
time: 438 us
  blocking collectives  173 us (39%)
  local copies, waits for them, and re-layouts  88.7 us (20%)
  waiting for transfers between devices  84.6 us (19%)
  matrix products  56.7 us (13%)
  other arithmetic  23.2 us (5%)
  starting transfers between devices  11.2 us (3%)
    all_to_all x1, blocking collectives, direct_path(): lax.all_to_all(update, 'ang', split_axis=1, concat_axis=2, tiled=True)  102 us
    all_to_all x1, waiting for transfers between devices, direct_path(): lax.all_to_all(grads, 'ang', split_axis=2, concat_axis=1, tiled=True)  84.6 us
    psum x1, blocking collectives, normalize(): totals = lax.psum(square_sums, ('ang', 'pix'))  70.5 us
    dot_general x5, matrix products, split_einsum(): jnp.einsum(form, left_piece, right_piece, preferred_element_type=jnp.floa...  56.7 us
    convert_element_type x1, local copies, waits for them, and re-layouts, direct_path(): update.astype(jnp.bfloat16).reshape(2, angle_count, row_local, col_count)  32.6 us
    unnamed x20, local copies, waits for them, and re-layouts  28 us
    cos x1, other arithmetic, phase_pair(): return (jnp.cos(radians), jnp.sin(radians))  18 us
    all_to_all x1, starting transfers between devices, direct_path(): lax.all_to_all(grads, 'ang', split_axis=2, concat_axis=1, tiled=True)  11.2 us
  transfers between devices with their start and end apart: 1, of which 1 were waited for; matrix products, arithmetic and copies ran while one was open for 4% of the time, Pallas kernels for 0%

commit v1 on v0

--- a/solution.py
+++ b/solution.py
@@ -32,7 +32,9 @@
 
 def normalize(coef_re, coef_im, weight, cell_count):
     square_sums = jnp.sum(weight[None, :] * (coef_re * coef_re + coef_im * coef_im), axis=1)
-    totals = lax.psum(square_sums, ("ang", "pix"))
+    totals = square_sums
+    for jj in ("ang", "pix"):
+        totals = jax.lax.psum(totals, jj)
     harmonic_rms = jnp.sqrt(totals / cell_count + 1e-06)
     factor = weight[None, :] / harmonic_rms[:, None]
     return (coef_re * factor, coef_im * factor, harmonic_rms)

time: 438 us -> 521 us (1.19)
  blocking collectives: 173 us -> 255 us
    psum x1 -> x2, blocking collectives: 70.5 us -> 148 us  [normalize(): totals = jax.lax.psum(totals, jj)]
where the time goes in v1:
time: 521 us; the launch traced here: 520 us
  blocking collectives  255 us (49%)
  local copies, waits for them, and re-layouts  88.7 us (17%)
  waiting for transfers between devices  84.6 us (16%)
  matrix products  56.6 us (11%)
  other arithmetic  23.2 us (4%)
  starting transfers between devices  11.2 us (2%)
    psum x2, blocking collectives, normalize(): totals = jax.lax.psum(totals, jj)  148 us
    all_to_all x1, blocking collectives, direct_path(): lax.all_to_all(update, 'ang', split_axis=1, concat_axis=2, tiled=True)  107 us
    all_to_all x1, waiting for transfers between devices, direct_path(): lax.all_to_all(grads, 'ang', split_axis=2, concat_axis=1, tiled=True)  84.6 us
    dot_general x5, matrix products, split_einsum(): jnp.einsum(form, left_piece, right_piece, preferred_element_type=jnp.floa...  56.6 us
    convert_element_type x1, local copies, waits for them, and re-layouts, direct_path(): update.astype(jnp.bfloat16).reshape(2, angle_count, row_local, col_count)  32.6 us
    unnamed x20, local copies, waits for them, and re-layouts  28 us
    cos x1, other arithmetic, phase_pair(): return (jnp.cos(radians), jnp.sin(radians))  18 us
    all_to_all x1, starting transfers between devices, direct_path(): lax.all_to_all(grads, 'ang', split_axis=2, concat_axis=1, tiled=True)  11.2 us
  transfers between devices with their start and end apart: 1, of which 1 were waited for; matrix products, arithmetic and copies ran while one was open for 4% of the time, Pallas kernels for 0%

profile of v1, /device:TPU:1, one launch (start us, length us, event | category | flops | bytes accessed | tf_op | source)
XLA Modules:
  0.0 520.3 jit_solution(9999730086849351772)
XLA Ops:
  0.6 11.5 %copy.18 = bf16[2,64,64,512]{3,1,0,2:T(8,128)(2,1)} copy(bf16[2,64,64,512]{3,2,1,0:T(8,128)(2,1)} %param.4) | data formatting | bytes 16777216 | tf_op args[0]
  12.1 0.0 copy-start.6
  12.1 0.0 copy-start.8
  12.1 11.2 %all-to-all-start = ((bf16[2,64,64,512]{3,1,0,2:T(8,128)(2,1)}), bf16[2,64,64,512]{3,1,0,2:T(8,128)(2,1)}, u32[]{:S(2)}, u32[]{:S(2)}) async-start(bf16[2,64,64,512]{3,1,0,2:T(8,128)(2,1)} %copy.18), calls=%async_computation | async-start | bytes 16777216 | tf_op jit(solution)/shard_map/all_to_all | solution.py:46
  23.3 0.7 dynamic-slice_convert_fusion
  24.1 0.0 copy-done.6
  24.1 0.0 copy-done.8
  24.1 18.0 %fusion.8 = (f32[256,4096]{1,0:T(8,128)}, f32[256,4096]{1,0:T(8,128)}) fusion(s32[4096]{0:T(1024)S(1)} %copy-done.6, s32[256]{0:T(256)S(1)} %copy-done.8), kind=kLoop, calls=%fused_computation.23 | loop fusion | flops 14680064 | bytes 8406016 | tf_op jit(solution)/shard_map/cos | solution.py:10
  42.1 84.6 %all-to-all-done = bf16[2,64,64,512]{3,1,0,2:T(8,128)(2,1)} async-done(((bf16[2,64,64,512]{3,1,0,2:T(8,128)(2,1)}), bf16[2,64,64,512]{3,1,0,2:T(8,128)(2,1)}, u32[]{:S(2)}, u32[]{:S(2)}) %all-to-all-start) | async-done | bytes 8388640 | tf_op jit(solution)/shard_map/all_to_all | solution.py:46
  126.7 7.9 %copy.24 = bf16[2,64,64,512]{3,1,2,0:T(8,128)(2,1)} copy(bf16[2,64,64,512]{3,1,0,2:T(8,128)(2,1)} %all-to-all-done) | data formatting | bytes 16777216 | tf_op jit(solution)/shard_map/all_to_all | solution.py:46
  134.6 0.0 copy-start
  134.6 0.0 copy-start.2
  134.6 5.4 %fusion.27 = (bf16[1,64,64,1,512]{4,2,1,3,0:T(8,128)(2,1)S(1)}, bf16[1,64,64,1,512]{4,2,1,3,0:T(8,128)(2,1)}) fusion(bf16[2,64,64,1,512]{4,2,1,3,0:T(8,128)(2,1)} %bitcast.17), kind=kLoop, calls=%fused_computation.41 | loop fusion | bytes 16777216 | tf_op jit(solution)/shard_map/slice | solution.py:53
  140.0 0.0 copy-start.5
  140.0 2.1 copy-done.5
  142.1 0.0 copy-done
  142.1 1.5 copy-done.2
  143.6 8.0 %fusion.2 = f32[512,1024]{1,0:T(8,128)} fusion(bf16[4096,512]{1,0:T(8,128)(2,1)} %bitcast.21, bf16[4096,512]{1,0:T(8,128)(2,1)S(1)} %bitcast.19, f32[256,4096]{1,0:T(8,128)S(1)} %copy-done.2, f32[256,4096]{1,0:T(8,128)S(1)} %copy-done), kind=kOutput, calls=%fused_computation.15 | convolution fusion | flops 4322230272 | bytes 18874368 | tf_op jit(solution)/shard_map/ka,ap->kp/dot_general | solution.py:28
  151.6 8.5 %fusion.9 = f32[512,1024]{1,0:T(8,128)S(1)} fusion(f32[512,1024]{1,0:T(8,128)} %fusion.2, bf16[4096,512]{1,0:T(8,128)(2,1)} %bitcast.22, bf16[4096,512]{1,0:T(8,128)(2,1)} %bitcast.20, f32[256,4096]{1,0:T(8,128)S(1)} %copy-done.2, f32[256,4096]{1,0:T(8,128)S(1)} %copy-done), kind=kOutput, calls=%fused_computation.24 | convolution fusion | flops 4320657408 | bytes 20971520 | tf_op jit(solution)/shard_map/ka,ap->kp/dot_general | solution.py:28
  160.1 0.0 copy-start.4
  160.2 1.3 copy-done.4
  161.5 0.2 multiply_reduce_fusion
  161.7 142.8 %psum.14 = f32[256]{0:T(256)S(1)} all-reduce(f32[256]{0:T(256)S(1)} %multiply_reduce_fusion), channel_id=1, replica_groups=mesh['ang'=64,'pix'=2] {'ang'}, use_global_device_ids=true, to_apply=%region_1.2 | all-reduce | flops 256 | bytes 2048 | tf_op jit(solution)/shard_map/psum | solution.py:37
  304.5 5.5 %psum.15 = f32[256]{0:T(256)S(1)} all-reduce(f32[256]{0:T(256)S(1)} %psum.14), channel_id=1, replica_groups=mesh['ang'=64,'pix'=2] {'pix'}, use_global_device_ids=true, to_apply=%region_2.3 | all-reduce | flops 256 | bytes 2048 | tf_op jit(solution)/shard_map/psum | solution.py:37
  310.0 0.0 copy-start.7
  310.0 1.7 fusion.26
  311.8 0.0 copy-start.1
  311.8 0.0 copy-start.3
  311.8 12.6 %fusion.11 = f32[4096,1024]{1,0:T(8,128)} fusion(f32[256,512]{1,0:T(8,128)S(1)} %get-tuple-element.12, f32[256,512]{1,0:T(8,128)S(1)} %get-tuple-element.7, f32[256,512]{1,0:T(8,128)S(1)} %get-tuple-element.6, f32[256,4096]{1,0:T(8,128)} %get-tuple-element.14, f32[256,4096]{1,0:T(8,128)} %get-tuple-element.13), kind=kOutput, calls=%fused_computation.26 | convolution fusion | flops 4307025920 | bytes 26738688 | tf_op jit(solution)/shard_map/ka,kp->ap/dot_general | solution.py:28
  324.4 0.0 copy-done.7
  324.4 0.0 copy-done.1
  324.4 0.0 copy-done.3
  324.4 8.2 %fusion.19 = f32[4096,1024]{1,0:T(8,128)} fusion(f32[256,512]{1,0:T(8,128)S(1)} %get-tuple-element.12, f32[256,512]{1,0:T(8,128)S(1)} %get-tuple-element.7, f32[256,512]{1,0:T(8,128)S(1)} %get-tuple-element.6, f32[256,4096]{1,0:T(8,128)S(1)} %copy-done.3, f32[256,4096]{1,0:T(8,128)S(1)} %copy-done.1), kind=kOutput, calls=%fused_computation.39 | convolution fusion | flops 4307550208 | bytes 26738688 | tf_op jit(solution)/shard_map/ka,kp->ap/dot_general | solution.py:28
  332.6 19.2 %add_add_fusion = f32[4096,1024]{1,0:T(8,128)} fusion(f32[4096,1024]{1,0:T(8,128)} %fusion.19, f32[4096,1024]{1,0:T(8,128)} %fusion.11, f32[256,512]{1,0:T(8,128)S(1)} %get-tuple-element.12, f32[256,512]{1,0:T(8,128)S(1)} %get-tuple-element.7, f32[256,512]{1,0:T(8,128)S(1)} %get-tuple-element.6, f32[256,4096]{1,0:T(8,128)} %get-tuple-element.14, ...), kind=kOutput, calls=%fused_computation.2 | convolution fusion | flops 4318035968 | bytes 60293120 | tf_op jit(solution)/shard_map/ka,kp->ap/dot_general | solution.py:28
  351.8 6.9 %slice_bitcast_fusion.1 = (f32[1,4096,1,512]{3,1,2,0:T(8,128)S(1)}, f32[1,4096,1,512]{3,1,2,0:T(8,128)S(1)}) fusion(f32[4096,1024]{1,0:T(8,128)} %add_add_fusion), kind=kLoop, calls=%fused_computation.4 | loop fusion | bytes 33554432 | tf_op jit(solution)/shard_map/stack | solution.py:63
  358.7 2.5 fusion
  361.2 32.6 %copy.20 = bf16[2,4096,1,512]{3,0,2,1:T(2,128)(2,1)S(1)} copy(bf16[2,4096,1,512]{3,1,2,0:T(8,128)(2,1)S(1)} %fusion) | data formatting | bytes 16777216 | tf_op jit(solution)/shard_map/convert_element_type | solution.py:64
  393.8 107.0 %all_to_all.33 = bf16[2,4096,1,512]{3,0,2,1:T(2,128)(2,1)} all-to-all(bf16[2,4096,1,512]{3,0,2,1:T(2,128)(2,1)S(1)} %copy.20), channel_id=1, replica_groups=mesh['ang'=64,'pix'=2] {'ang'}, dimensions={1} | all-to-all | bytes 16777216 | tf_op jit(solution)/shard_map/all_to_all | solution.py:65
  500.8 8.0 %copy.21 = bf16[2,4096,1,512]{3,1,0,2:T(8,128)(2,1)} copy(bf16[2,4096,1,512]{3,0,2,1:T(2,128)(2,1)} %all_to_all.33) | data formatting | bytes 16777216 | tf_op jit(solution)/shard_map/all_to_all | solution.py:65
  508.7 11.5 %copy.22 = bf16[2,64,64,512]{3,2,1,0:T(8,128)(2,1)} copy(bf16[2,64,64,512]{3,1,2,0:T(8,128)(2,1)} %bitcast.18) | data formatting | bytes 16777216
  (1 shorter events, 0.0 us)
Async XLA Ops:
  12.1 11.9 %copy-start.6 = (s32[4096]{0:T(1024)S(1)}, s32[4096]{0:T(1024)}, u32[]{:S(2)}) copy-start(s32[4096]{0:T(1024)} %param.5) | copy-start | bytes 49156
  12.1 11.9 %copy-start.8 = (s32[256]{0:T(256)S(1)}, s32[256]{0:T(256)}, u32[]{:S(2)}) copy-start(s32[256]{0:T(256)} %param.6) | copy-start | bytes 3076
  12.1 114.6 %all-to-all-start = ((bf16[2,64,64,512]{3,1,0,2:T(8,128)(2,1)}), bf16[2,64,64,512]{3,1,0,2:T(8,128)(2,1)}, u32[]{:S(2)}, u32[]{:S(2)}) async-start(bf16[2,64,64,512]{3,1,0,2:T(8,128)(2,1)} %copy.18), calls=%async_computation | async-start | bytes 16777216 | tf_op jit(solution)/shard_map/all_to_all | solution.py:46
  134.6 7.5 %copy-start = (f32[256,4096]{1,0:T(8,128)S(1)}, f32[256,4096]{1,0:T(8,128)}, u32[]{:S(2)}) copy-start(f32[256,4096]{1,0:T(8,128)} %get-tuple-element.13) | copy-start | bytes 12582916
  134.6 9.0 %copy-start.2 = (f32[256,4096]{1,0:T(8,128)S(1)}, f32[256,4096]{1,0:T(8,128)}, u32[]{:S(2)}) copy-start(f32[256,4096]{1,0:T(8,128)} %get-tuple-element.14) | copy-start | bytes 12582916
  140.0 2.1 copy-start.5
  160.1 1.3 copy-start.4
  310.0 14.4 %copy-start.7 = (f32[256]{0:T(256)}, f32[256]{0:T(256)S(1)}, u32[]{:S(2)}) copy-start(f32[256]{0:T(256)S(1)} %add_sqrt_fusion) | copy-start | bytes 3076
  311.8 12.7 %copy-start.1 = (f32[256,4096]{1,0:T(8,128)S(1)}, f32[256,4096]{1,0:T(8,128)}, u32[]{:S(2)}) copy-start(f32[256,4096]{1,0:T(8,128)} %get-tuple-element.13) | copy-start | bytes 12582916
  311.8 12.7 %copy-start.3 = (f32[256,4096]{1,0:T(8,128)S(1)}, f32[256,4096]{1,0:T(8,128)}, u32[]{:S(2)}) copy-start(f32[256,4096]{1,0:T(8,128)} %get-tuple-element.14) | copy-start | bytes 12582916
